TPU v7x, 256 devices: a whole 4x4x8 slice. The times are simulated.
256 devices in a mesh: row: 8 (over z), col: 32 (over x, y, core).
Axes of the slice: x: 4, y: 4, z: 8, core: 2. Of those that a mesh axis runs over, the one named last changes fastest.
Arguments:
- tile_values: float32 [8, 32, 128, 128, 128], P('row', 'col')
- tile_coords: int32 [8, 32, 128, 2], P('row', 'col'), may hold values from 0 to 271, as said below
- tile_count: int32 [8, 32], P('row', 'col'), may hold values from 16 to 128, as said below
- objective: float32 [262144], P('col')
- lower: float32 [262144], P('col'), may hold values from -2 to -0.2
- upper: float32 [262144], P('col'), may hold values from 0.2 to 2
- rhs: float32 [278528], P('row')
- primal_start: float32 [262144], P('col'), may hold values from -4 to 4
- dual_start: float32 [278528], P('row'), may hold values from 0 to 1
- step_size: float32 [1], replicated, may hold values from 0.02 to 0.06
Outputs:
- primal_solution: float32 [262144], P('col')
- dual_solution: float32 [278528], P('row')
Inputs may be any that keep to these rules, and one draw needn't show every extreme that they name: `tile_coords`: coordinates are local: block rows 0 to 271, block columns 0 to 63, also in unused slots. Devices whose col index is congruent to their row index modulo the size of row hold one period: their block rows are (col index // size of row) * 64 plus 0 to 63. All other devices hold only linking block rows, 256 to 271. Every block row and every block column of A is met by some used slot. `tile_count`: period devices use all slots; other devices use 16 to 64 slots.
All inputs are finite; a program needn't handle non-finite values.
Results may differ from a plain program's by a relative error of at most 0.00012.
Values sent between devices are 32-bit elements; how exact they have to be, the bound alone decides.
No kernel may reach another device: no remote copies, remote signals or barrier semaphores. Data moves between devices by JAX's collectives and lax.ppermute only.
A program may use at most 64 MiB of HBM per device.

v0:
```python
import jax
import jax.numpy as jnp
from jax import lax
from jax.sharding import PartitionSpec as P

RUIZ = 2
ITERS = 2
EPSILON = 1e-06
HIGHEST = lax.Precision.HIGHEST


def local(
    tile_values,
    tile_coords,
    tile_count,
    objective,
    lower,
    upper,
    rhs,
    primal_start,
    dual_start,
    step_size,
):
    tile_width = tile_values.shape[-1]
    slot_count = tile_values.shape[2]
    matrix = tile_values.reshape(slot_count, tile_width, tile_width)
    coords = tile_coords.reshape(slot_count, 2)
    block_rows = coords[:, 0]
    block_cols = coords[:, 1]
    row_blocks = rhs.shape[0] // tile_width
    col_blocks = objective.shape[0] // tile_width
    in_use = (jnp.arange(slot_count, dtype=jnp.int32) < tile_count.reshape(())).astype(jnp.float32)
    row_onehot = (jnp.arange(row_blocks, dtype=jnp.int32)[:, None] == block_rows[None, :]).astype(
        jnp.float32
    ) * in_use[None, :]
    col_onehot = (jnp.arange(col_blocks, dtype=jnp.int32)[:, None] == block_cols[None, :]).astype(
        jnp.float32
    ) * in_use[None, :]
    magnitude = jnp.abs(matrix) * in_use[:, None, None]
    row_scale = jnp.ones((row_blocks, tile_width), jnp.float32)
    col_scale = jnp.ones((col_blocks, tile_width), jnp.float32)
    for sweep in range(RUIZ):
        col_pieces = jnp.take(col_scale, block_cols, axis=0)
        row_pieces = jnp.take(row_scale, block_rows, axis=0)
        row_local = jnp.max(magnitude * col_pieces[:, None, :], axis=2)
        col_local = jnp.max(magnitude * row_pieces[:, :, None], axis=1)
        row_peak = jnp.zeros((row_blocks, tile_width), jnp.float32).at[block_rows].max(row_local)
        col_peak = jnp.zeros((col_blocks, tile_width), jnp.float32).at[block_cols].max(col_local)
        peak_target = row_peak
        peak_joined = lax.pmax(peak_target, "col")
        row_peak = peak_joined
        col_peak = lax.pmax(col_peak, "row")
        row_scale = row_scale / jnp.sqrt(row_scale * row_peak + EPSILON)
        col_scale = col_scale / jnp.sqrt(col_scale * col_peak + EPSILON)
    cost = col_scale * objective.reshape(col_blocks, tile_width)
    bound = row_scale * rhs.reshape(row_blocks, tile_width)
    low_scaled = lower.reshape(col_blocks, tile_width) / col_scale
    high_scaled = upper.reshape(col_blocks, tile_width) / col_scale
    primal = primal_start.reshape(col_blocks, tile_width) / col_scale
    dual = dual_start.reshape(row_blocks, tile_width) / row_scale
    cost_square = jnp.sum(cost * cost)
    bound_square = jnp.sum(bound * bound)
    cost_total = lax.psum(cost_square, "col")
    bound_total = lax.psum(bound_square, "row")
    weight = jnp.sqrt(cost_total + EPSILON) / jnp.sqrt(bound_total + EPSILON)
    primal_step = step_size[0] / weight
    dual_step = step_size[0] * weight
    for iteration in range(ITERS):
        pieces = jnp.take(row_scale * dual, block_rows, axis=0)
        products = jnp.einsum("tij,ti->tj", matrix, pieces, precision=HIGHEST)
        image = lax.psum(jnp.dot(col_onehot, products, precision=HIGHEST), "row")
        moved = jnp.clip(primal - primal_step * (cost - col_scale * image), low_scaled, high_scaled)
        extra = 2.0 * moved - primal
        forward_pieces = jnp.take(col_scale * extra, block_cols, axis=0)
        forward_products = jnp.einsum("tij,tj->ti", matrix, forward_pieces, precision=HIGHEST)
        partial_rows = jnp.dot(row_onehot, forward_products, precision=HIGHEST)
        total = lax.psum(partial_rows, "col")
        dual = jnp.maximum(dual + dual_step * (bound - row_scale * total), 0.0)
        primal = moved
    return ((col_scale * primal).reshape(-1), (row_scale * dual).reshape(-1))


def solution(mesh):
    placed = (
        P("row", "col", None, None, None),
        P("row", "col", None, None),
        P("row", "col"),
        P("col"),
        P("col"),
        P("col"),
        P("row"),
        P("col"),
        P("row"),
        P(),
    )
    return jax.shard_map(
        local, mesh=mesh, in_specs=placed, out_specs=(P("col"), P("row")), check_vma=False
    )
```

profile of v0, /device:TPU:1, one launch (start us, length us, event | category | flops | bytes accessed | tf_op | source)
XLA Modules:
  0.0 609.2 jit_solution(8344150141682839794)
XLA Ops:
  7.2 0.0 all-reduce.10.cloned.1.call-start
  7.2 0.8 compare_and_fusion
  8.0 0.8 slice_bitcast_fusion
  9.4 0.6 gather_fusion
  10.1 0.1 broadcast_select_fusion.7
  10.2 5.7 multiply_reduce_fusion.3
  15.9 1.0 scatter_custom_fusion
  16.9 26.6 %pmax.28 = f32[64,128]{1,0:T(8,128)S(1)} all-reduce(f32[64,128]{1,0:T(8,128)S(1)} %scatter_custom_fusion), channel_id=1, replica_groups=mesh['row'=8,'col'=32] {'row'}, use_global_device_ids=true, to_apply=%region_2.4 | all-reduce | flops 8192 | bytes 65536 | tf_op jit(solution)/shard_map/pmax | solution.py:52
  43.5 0.6 gather_fusion.3
  44.2 0.6 gather_fusion.1
  44.8 0.1 broadcast_select_fusion.6
  44.9 7.3 %multiply_reduce_fusion = (f32[128,128]{1,0:T(8,128)S(1)}, f32[128,128]{1,0:T(8,128)S(1)}) fusion(f32[1,1,128,128,128]{4,3,2,1,0:T(8,128)} %param.14, f32[128,128]{1,0:T(8,128)S(1)} %get-tuple-element.30, f32[128]{0:T(128)S(1)} %compare_convert_fusion, f32[128,128]{1,0:T(8,128)S(1)} %get-tuple-element.29), kind=kLoop, calls=%fused_computation.22 | loop fusion | flops 12550144 | bytes 8651264 | tf_op jit(solution)/shard_map/reduce_max | solution.py:45
  52.2 1.6 scatter_custom_fusion.3
  53.8 1.6 scatter_custom_fusion.1
  55.5 0.0 all-reduce.10.cloned.1.call-update
  55.5 0.0 all-reduce.6.cloned.1.call-start
  56.2 116.2 %all-reduce.10.cloned.1.call-done = (f32[272,128]{1,0:T(8,128)}, f32[272,128]{1,0:T(8,128)}) async-done(((f32[272,128]{1,0:T(8,128)}, f32[272,128]{1,0:T(8,128)}), (f32[272,128]{1,0:T(8,128)}, f32[272,128]{1,0:T(8,128)})) %all-reduce.10.cloned.1.call-update) | async-done | bytes 278544 | tf_op jit(solution)/shard_map/pmax | solution.py:50
  172.4 1.6 multiply_reduce_fusion.4
  174.0 0.6 gather_fusion.4
  174.7 0.6 gather_fusion.2
  175.3 0.1 broadcast_select_fusion.3
  175.5 9.4 %fusion.6 = f32[128,1,128]{2,1,0:T(1,128)S(1)} fusion(f32[128,128,1]{1,2,0:T(1,128)S(1)} %bitcast.129, f32[1,1,128,128,128]{4,3,2,1,0:T(8,128)} %param.14), kind=kOutput, calls=%fused_computation.18 | convolution fusion | flops 25165824 | bytes 8519680 | tf_op jit(solution)/shard_map/tij,ti->tj/dot_general | solution.py:70
  184.9 0.2 fusion.27
  185.1 24.6 %all-reduce.1 = (f32[64,128]{1,0:T(8,128)S(1)}, f32[]{:T(128)}) all-reduce(f32[64,128]{1,0:T(8,128)S(1)} %fusion.27, f32[]{:T(128)} %get-tuple-element.12), channel_id=1, replica_groups=mesh['row'=8,'col'=32] {'row'}, use_global_device_ids=true, to_apply=%region_16.19 | all-reduce | flops 8193 | bytes 65544 | tf_op jit(solution)/shard_map/psum | solution.py:71
  210.3 5.7 multiply_reduce_fusion.1
  216.0 1.0 scatter_custom_fusion.2
  217.1 20.4 %pmax.30 = f32[64,128]{1,0:T(8,128)S(1)} all-reduce(f32[64,128]{1,0:T(8,128)S(1)} %scatter_custom_fusion.2), channel_id=1, replica_groups=mesh['row'=8,'col'=32] {'row'}, use_global_device_ids=true, to_apply=%region_8.11 | all-reduce | flops 8192 | bytes 65536 | tf_op jit(solution)/shard_map/pmax | solution.py:52
  237.4 0.6 multiply_reduce_fusion.5
  238.0 77.9 %psum.42 = f32[]{:T(128)} all-reduce(f32[]{:T(128)} %get-tuple-element.10), channel_id=1, replica_groups=mesh['row'=8,'col'=32] {'col'}, use_global_device_ids=true, to_apply=%region_10.13 | all-reduce | flops 1 | bytes 8 | tf_op jit(solution)/shard_map/psum | solution.py:63
  316.8 0.6 gather_fusion.5
  317.4 0.1 broadcast_select_fusion.2
  317.5 15.4 %fusion.4 = f32[128,1,128]{2,1,0:T(1,128)S(1)} fusion(f32[128,128,1]{1,2,0:T(1,128)S(1)} %bitcast.128, f32[1,1,128,128,128]{4,3,2,1,0:T(8,128)} %param.14), kind=kOutput, calls=%fused_computation.16 | convolution fusion | flops 25165824 | bytes 8519680 | tf_op jit(solution)/shard_map/tij,tj->ti/dot_general | solution.py:75
  332.9 0.9 fusion.11
  333.8 0.0 all-reduce.8.cloned.1.call-start
  333.9 103.0 %all-reduce.6.cloned.1.call-done = f32[272,128]{1,0:T(8,128)} async-done(((f32[272,128]{1,0:T(8,128)}), f32[272,128]{1,0:T(8,128)}) %all-reduce.6.cloned.1.call-update) | async-done | bytes 139280 | tf_op jit(solution)/shard_map/psum | solution.py:77
  436.9 1.0 fusion.13
  437.8 0.6 gather_fusion.6
  438.5 0.1 broadcast_select_fusion.1
  438.6 9.4 %fusion.2 = f32[128,1,128]{2,1,0:T(1,128)S(1)} fusion(f32[128,128,1]{1,2,0:T(1,128)S(1)} %bitcast.124, f32[1,1,128,128,128]{4,3,2,1,0:T(8,128)} %param.14), kind=kOutput, calls=%fused_computation.14 | convolution fusion | flops 25165824 | bytes 8519680 | tf_op jit(solution)/shard_map/tij,ti->tj/dot_general | solution.py:70
  448.0 0.2 fusion.25
  448.2 23.4 %psum.46 = f32[64,128]{1,0:T(8,128)S(1)} all-reduce(f32[64,128]{1,0:T(8,128)S(1)} %fusion.25), channel_id=1, replica_groups=mesh['row'=8,'col'=32] {'row'}, use_global_device_ids=true, to_apply=%region_18.21 | all-reduce | flops 8192 | bytes 65536 | tf_op jit(solution)/shard_map/psum | solution.py:71
  471.5 0.6 subtract_multiply_fusion
  472.2 0.6 gather_fusion.7
  472.8 0.1 broadcast_select_fusion
  472.9 15.4 %fusion = f32[128,1,128]{2,1,0:T(1,128)S(1)} fusion(f32[128,128,1]{1,2,0:T(1,128)S(1)} %bitcast.126, f32[1,1,128,128,128]{4,3,2,1,0:T(8,128)} %param.14), kind=kOutput, calls=%fused_computation.12 | convolution fusion | flops 25165824 | bytes 8519680 | tf_op jit(solution)/shard_map/tij,tj->ti/dot_general | solution.py:75
  488.3 0.9 fusion.9
  489.3 111.7 %all-reduce.8.cloned.1.call-done = f32[272,128]{1,0:T(8,128)} async-done(((f32[272,128]{1,0:T(8,128)}), f32[272,128]{1,0:T(8,128)}) %all-reduce.8.cloned.1.call-update) | async-done | bytes 139280 | tf_op jit(solution)/shard_map/psum | solution.py:77
  601.0 1.6 multiply_bitcast_fusion
  (24 shorter events, 0.2 us)
Async XLA Ops:
  7.2 165.2 %all-reduce.10.cloned.1.call-start = ((), (), s32[]{:S(2)}) async-start(), calls=%async_computation.2 | async-start | bytes 557056 | tf_op jit(solution)/shard_map/pmax | solution.py:50
  10.2 162.2 %copy-start = (f32[34816]{0:T(1024)S(1)}, f32[34816]{0:T(1024)}, u32[]{:S(2)}) copy-start(f32[34816]{0:T(1024)} %param.20) | copy-start | bytes 417796
  10.2 163.8 %copy-start.1 = (f32[34816]{0:T(1024)S(1)}, f32[34816]{0:T(1024)}, u32[]{:S(2)}) copy-start(f32[34816]{0:T(1024)} %param.22) | copy-start | bytes 417796
  55.5 381.4 %all-reduce.6.cloned.1.call-start = ((), (), s32[]{:S(2)}) async-start(), calls=%async_computation | async-start | bytes 278528 | tf_op jit(solution)/shard_map/psum | solution.py:77
  175.4 62.0 %copy-start.3 = (f32[8192]{0:T(1024)S(1)}, f32[8192]{0:T(1024)}, u32[]{:S(2)}) copy-start(f32[8192]{0:T(1024)} %param.17) | copy-start | bytes 98308
  175.4 141.3 %copy-start.4 = (f32[8192]{0:T(1024)S(1)}, f32[8192]{0:T(1024)}, u32[]{:S(2)}) copy-start(f32[8192]{0:T(1024)} %param.19) | copy-start | bytes 98308
  175.4 141.3 %copy-start.5 = (f32[8192]{0:T(1024)S(1)}, f32[8192]{0:T(1024)}, u32[]{:S(2)}) copy-start(f32[8192]{0:T(1024)} %param.18) | copy-start | bytes 98308
  175.5 141.3 %copy-start.6 = (f32[8192]{0:T(1024)S(1)}, f32[8192]{0:T(1024)}, u32[]{:S(2)}) copy-start(f32[8192]{0:T(1024)} %param.21) | copy-start | bytes 98308
  333.8 267.1 %all-reduce.8.cloned.1.call-start = ((), (), s32[]{:S(2)}) async-start(), calls=%async_computation.1 | async-start | bytes 278528 | tf_op jit(solution)/shard_map/psum | solution.py:77
  438.6 162.4 %copy-start.2 = (f32[272,128]{1,0:T(8,128)S(1)}, f32[272,128]{1,0:T(8,128)}, u32[]{:S(2)}) copy-start(f32[272,128]{1,0:T(8,128)} %all-reduce.6.cloned.1.call-done) | copy-start | bytes 417796
Sparse Core Ops, SparseCore 0:
  55.6 116.7 all-reduce.9
  334.0 102.8 all-reduce.5
  489.4 111.5 all-reduce.7
where the time goes:
time: 610 us; the launch traced here: 609 us
  waiting for transfers between devices  331 us (54%)
  blocking collectives  173 us (28%)
  matrix products  51.8 us (8%)
  other arithmetic  31.6 us (5%)
  between operations  16.7 us (3%)
    psum x2, waiting for transfers between devices, local(): total = lax.psum(partial_rows, 'col')  215 us
    pmax x1, waiting for transfers between devices, local(): peak_joined = lax.pmax(peak_target, 'col')  116 us
    psum x1, blocking collectives, local(): cost_total = lax.psum(cost_square, 'col')  77.9 us
    psum x2, blocking collectives, local(): image = lax.psum(jnp.dot(col_onehot, products, precision=HIGHEST), 'row')  47.9 us
    pmax x2, blocking collectives, local(): col_peak = lax.pmax(col_peak, 'row')  46.9 us
    dot_general x2, matrix products, local(): jnp.einsum('tij,tj->ti', matrix, forward_pieces, precision=HIGHEST)  30.8 us
    dot_general x2, matrix products, local(): products = jnp.einsum('tij,ti->tj', matrix, pieces, precision=HIGHEST)  18.8 us
  transfers between devices with their start and end apart: 3, of which 3 were waited for; matrix products, arithmetic and copies ran while one was open for 0% of the time, Pallas kernels for 0%

commit v1 on v0

--- a/solution.py
+++ b/solution.py
@@ -74,7 +74,9 @@
         forward_pieces = jnp.take(col_scale * extra, block_cols, axis=0)
         forward_products = jnp.einsum("tij,tj->ti", matrix, forward_pieces, precision=HIGHEST)
         partial_rows = jnp.dot(row_onehot, forward_products, precision=HIGHEST)
-        total = lax.psum(partial_rows, "col")
+        total = partial_rows
+        for hop in (1, 2, 4, 8, 16):
+            total = total + lax.ppermute(total, "col", [(dev, dev ^ hop) for dev in range(32)])
         dual = jnp.maximum(dual + dual_step * (bound - row_scale * total), 0.0)
         primal = moved
     return ((col_scale * primal).reshape(-1), (row_scale * dual).reshape(-1))

time: 610 us -> 449 us (0.74)
  waiting for transfers between devices: 331 us -> 157 us
  starting transfers between devices: 0.12 us -> 21.8 us
  blocking collectives: 173 us -> 164 us
    psum x2 -> x0, waiting for transfers between devices: 215 us -> none  [local(): total = lax.psum(partial_rows, 'col')]
    ppermute x0 -> x10, waiting for transfers between devices: none -> 41.1 us  [local(): lax.ppermute(total, 'col', [(dev, dev ^ hop) for dev in range(32)])]
    ppermute x0 -> x10, starting transfers between devices: none -> 21.8 us  [local(): lax.ppermute(total, 'col', [(dev, dev ^ hop) for dev in range(32)])]
    psum x1, blocking collectives: 77.9 us -> 70.8 us  [local(): cost_total = lax.psum(cost_square, 'col')]
  transfers between devices with their start and end apart: 3 -> 11, of which waited for: 3 -> 11; matrix products, arithmetic and copies ran while one was open for 0% -> 0% of each run, Pallas kernels for 0% -> 0%
where the time goes in v1:
time: 449 us; the launch traced here: 446 us
  blocking collectives  164 us (37%)
  waiting for transfers between devices  157 us (35%)
  matrix products  50.5 us (11%)
  other arithmetic  29.9 us (7%)
  starting transfers between devices  21.8 us (5%)
  between operations  17.1 us (4%)
  local copies, waits for them, and re-layouts  5.21 us (1%)
    pmax x1, waiting for transfers between devices, local(): peak_joined = lax.pmax(peak_target, 'col')  116 us
    psum x1, blocking collectives, local(): cost_total = lax.psum(cost_square, 'col')  70.8 us
    pmax x2, blocking collectives, local(): col_peak = lax.pmax(col_peak, 'row')  49.8 us
    psum x2, blocking collectives, local(): image = lax.psum(jnp.dot(col_onehot, products, precision=HIGHEST), 'row')  43.4 us
    ppermute x10, waiting for transfers between devices, local(): lax.ppermute(total, 'col', [(dev, dev ^ hop) for dev in range(32)])  41.1 us
    dot_general x2, matrix products, local(): jnp.einsum('tij,tj->ti', matrix, forward_pieces, precision=HIGHEST)  30.8 us
    ppermute x10, starting transfers between devices, local(): lax.ppermute(total, 'col', [(dev, dev ^ hop) for dev in range(32)])  21.8 us
    dot_general x2, matrix products, local(): products = jnp.einsum('tij,ti->tj', matrix, pieces, precision=HIGHEST)  18.8 us
  transfers between devices with their start and end apart: 11, of which 11 were waited for; matrix products, arithmetic and copies ran while one was open for 0% of the time, Pallas kernels for 0%

profile of v1, /device:TPU:1, one launch (start us, length us, event | category | flops | bytes accessed | tf_op | source)
XLA Modules:
  0.0 445.8 jit_solution(11676373317948062848)
XLA Ops:
  7.2 0.8 slice_bitcast_fusion
  8.0 0.8 compare_and_fusion
  9.4 0.6 gather_fusion
  10.2 5.7 %multiply_reduce_fusion.3 = f32[128,128]{1,0:T(8,128)S(1)} fusion(f32[1,1,128,128,128]{4,3,2,1,0:T(8,128)} %param.14, f32[128,128]{1,0:T(8,128)S(1)} %broadcast_select_fusion.7, f32[128]{0:T(128)S(1)} %compare_convert_fusion), kind=kLoop, calls=%fused_computation.25 | loop fusion | flops 8372224 | bytes 8520192 | tf_op jit(solution)/shard_map/reduce_max | solution.py:46
  15.9 1.0 scatter_custom_fusion
  17.0 26.6 %pmax.28 = f32[64,128]{1,0:T(8,128)S(1)} all-reduce(f32[64,128]{1,0:T(8,128)S(1)} %scatter_custom_fusion), channel_id=1, replica_groups=mesh['row'=8,'col'=32] {'row'}, use_global_device_ids=true, to_apply=%region_2.4 | all-reduce | flops 8192 | bytes 65536 | tf_op jit(solution)/shard_map/pmax | solution.py:52
  43.6 0.6 gather_fusion.1
  44.2 0.6 gather_fusion.3
  45.0 7.3 %multiply_reduce_fusion = (f32[128,128]{1,0:T(8,128)S(1)}, f32[128,128]{1,0:T(8,128)S(1)}) fusion(f32[1,1,128,128,128]{4,3,2,1,0:T(8,128)} %param.14, f32[128,128]{1,0:T(8,128)S(1)} %get-tuple-element.30, f32[128]{0:T(128)S(1)} %compare_convert_fusion, f32[128,128]{1,0:T(8,128)S(1)} %get-tuple-element.29), kind=kLoop, calls=%fused_computation.22 | loop fusion | flops 12550144 | bytes 8651264 | tf_op jit(solution)/shard_map/reduce_max | solution.py:45
  52.2 1.6 scatter_custom_fusion.3
  53.9 1.6 scatter_custom_fusion.1
  56.2 116.2 %all-reduce.4.cloned.1.call-done = (f32[272,128]{1,0:T(8,128)}, f32[272,128]{1,0:T(8,128)}) async-done(((f32[272,128]{1,0:T(8,128)}, f32[272,128]{1,0:T(8,128)}), (f32[272,128]{1,0:T(8,128)}, f32[272,128]{1,0:T(8,128)})) %all-reduce.4.cloned.1.call-update) | async-done | bytes 278544 | tf_op jit(solution)/shard_map/pmax | solution.py:50
  172.4 1.6 multiply_reduce_fusion.4
  174.0 0.6 gather_fusion.2
  174.7 0.6 gather_fusion.4
  175.5 9.4 %fusion.6 = f32[128,1,128]{2,1,0:T(1,128)S(1)} fusion(f32[128,128,1]{1,2,0:T(1,128)S(1)} %bitcast.131, f32[1,1,128,128,128]{4,3,2,1,0:T(8,128)} %param.14), kind=kOutput, calls=%fused_computation.18 | convolution fusion | flops 25165824 | bytes 8519680 | tf_op jit(solution)/shard_map/tij,ti->tj/dot_general | solution.py:70
  184.9 5.6 %multiply_reduce_fusion.1 = f32[128,128]{1,0:T(8,128)S(1)} fusion(f32[1,1,128,128,128]{4,3,2,1,0:T(8,128)} %param.14, f32[128,128]{1,0:T(8,128)S(1)} %get-tuple-element.28, f32[128]{0:T(128)S(1)} %compare_convert_fusion), kind=kLoop, calls=%fused_computation.23 | loop fusion | flops 8372224 | bytes 8520192 | tf_op jit(solution)/shard_map/reduce_max | solution.py:46
  190.5 1.0 scatter_custom_fusion.2
  191.5 23.2 %pmax.30 = f32[64,128]{1,0:T(8,128)S(1)} all-reduce(f32[64,128]{1,0:T(8,128)S(1)} %scatter_custom_fusion.2), channel_id=1, replica_groups=mesh['row'=8,'col'=32] {'row'}, use_global_device_ids=true, to_apply=%region_8.11 | all-reduce | flops 8192 | bytes 65536 | tf_op jit(solution)/shard_map/pmax | solution.py:52
  214.7 0.6 multiply_reduce_fusion.5
  215.3 70.8 %psum.28 = f32[]{:T(128)} all-reduce(f32[]{:T(128)} %get-tuple-element.10), channel_id=1, replica_groups=mesh['row'=8,'col'=32] {'col'}, use_global_device_ids=true, to_apply=%region_10.13 | all-reduce | flops 1 | bytes 8 | tf_op jit(solution)/shard_map/psum | solution.py:63
  286.9 0.2 fusion.27
  287.1 21.8 %all-reduce.1 = (f32[64,128]{1,0:T(8,128)S(1)}, f32[]{:T(128)}) all-reduce(f32[64,128]{1,0:T(8,128)S(1)} %fusion.27, f32[]{:T(128)} %get-tuple-element.12), channel_id=1, replica_groups=mesh['row'=8,'col'=32] {'row'}, use_global_device_ids=true, to_apply=%region_16.19 | all-reduce | flops 8193 | bytes 65544 | tf_op jit(solution)/shard_map/psum | solution.py:71
  309.6 0.6 gather_fusion.5
  310.4 15.4 %fusion.4 = f32[128,1,128]{2,1,0:T(1,128)S(1)} fusion(f32[128,128,1]{1,2,0:T(1,128)S(1)} %bitcast.130, f32[1,1,128,128,128]{4,3,2,1,0:T(8,128)} %param.14), kind=kOutput, calls=%fused_computation.16 | convolution fusion | flops 25165824 | bytes 8519680 | tf_op jit(solution)/shard_map/tij,tj->ti/dot_general | solution.py:75
  325.8 0.3 fusion.11
  326.0 7.5 %collective-permute-start = (f32[272,128]{1,0:T(8,128)S(1)}, f32[272,128]{1,0:T(8,128)S(1)}, u32[]{:S(2)}, u32[]{:S(2)}) collective-permute-start(f32[272,128]{1,0:T(8,128)S(1)} %fusion.11), channel_id=1, source_target_pairs={{0,1},{1,0},{2,3},{3,2},{4,5},{5,4},{6,7},{7,6},{8,9},{9,8},{10,11... | collective-permute-start | bytes 417800 | tf_op jit(solution)/shard_map/ppermute | solution.py:79
  333.6 1.0 collective-permute-done
  334.7 4.9 %collective-permute-done.1 = f32[272,128]{1,0:T(8,128)S(1)} collective-permute-done((f32[272,128]{1,0:T(8,128)S(1)}, f32[272,128]{1,0:T(8,128)S(1)}, u32[]{:S(2)}, u32[]{:S(2)}) %collective-permute-start.1) | collective-permute-done | bytes 139296 | tf_op jit(solution)/shard_map/ppermute | solution.py:79
  339.7 5.4 %collective-permute-done.2 = f32[272,128]{1,0:T(8,128)S(1)} collective-permute-done((f32[272,128]{1,0:T(8,128)S(1)}, f32[272,128]{1,0:T(8,128)S(1)}, u32[]{:S(2)}, u32[]{:S(2)}) %collective-permute-start.2) | collective-permute-done | bytes 139296 | tf_op jit(solution)/shard_map/ppermute | solution.py:79
  345.2 3.9 collective-permute-done.3
  349.1 0.3 collective-permute-start.4
  349.4 5.4 %collective-permute-done.4 = f32[272,128]{1,0:T(8,128)S(1)} collective-permute-done((f32[272,128]{1,0:T(8,128)S(1)}, f32[272,128]{1,0:T(8,128)S(1)}, u32[]{:S(2)}, u32[]{:S(2)}) %collective-permute-start.4) | collective-permute-done | bytes 139296 | tf_op jit(solution)/shard_map/ppermute | solution.py:79
  354.9 0.6 gather_fusion.6
  355.6 9.4 %fusion.2 = f32[128,1,128]{2,1,0:T(1,128)S(1)} fusion(f32[128,128,1]{1,2,0:T(1,128)S(1)} %bitcast.127, f32[1,1,128,128,128]{4,3,2,1,0:T(8,128)} %param.14), kind=kOutput, calls=%fused_computation.14 | convolution fusion | flops 25165824 | bytes 8519680 | tf_op jit(solution)/shard_map/tij,ti->tj/dot_general | solution.py:70
  365.0 0.2 fusion.25
  365.2 21.6 %psum.31 = f32[64,128]{1,0:T(8,128)S(1)} all-reduce(f32[64,128]{1,0:T(8,128)S(1)} %fusion.25), channel_id=1, replica_groups=mesh['row'=8,'col'=32] {'row'}, use_global_device_ids=true, to_apply=%region_17.20 | all-reduce | flops 8192 | bytes 65536 | tf_op jit(solution)/shard_map/psum | solution.py:71
  386.8 0.6 subtract_multiply_fusion
  387.5 0.6 gather_fusion.7
  388.2 15.4 %fusion = f32[128,1,128]{2,1,0:T(1,128)S(1)} fusion(f32[128,128,1]{1,2,0:T(1,128)S(1)} %bitcast.129, f32[1,1,128,128,128]{4,3,2,1,0:T(8,128)} %param.14), kind=kOutput, calls=%fused_computation.12 | convolution fusion | flops 25165824 | bytes 8519680 | tf_op jit(solution)/shard_map/tij,tj->ti/dot_general | solution.py:75
  403.6 0.3 fusion.9
  403.9 13.3 %collective-permute-start.5 = (f32[272,128]{1,0:T(8,128)S(1)}, f32[272,128]{1,0:T(8,128)S(1)}, u32[]{:S(2)}, u32[]{:S(2)}) collective-permute-start(f32[272,128]{1,0:T(8,128)S(1)} %fusion.9), channel_id=1, source_target_pairs={{0,1},{1,0},{2,3},{3,2},{4,5},{5,4},{6,7},{7,6},{8,9},{9,8},{10,11... | collective-permute-start | bytes 417800 | tf_op jit(solution)/shard_map/ppermute | solution.py:79
  417.2 1.0 collective-permute-done.5
  418.3 4.9 %collective-permute-done.6 = f32[272,128]{1,0:T(8,128)S(1)} collective-permute-done((f32[272,128]{1,0:T(8,128)S(1)}, f32[272,128]{1,0:T(8,128)S(1)}, u32[]{:S(2)}, u32[]{:S(2)}) %collective-permute-start.6) | collective-permute-done | bytes 139296 | tf_op jit(solution)/shard_map/ppermute | solution.py:79
  423.3 5.4 %collective-permute-done.7 = f32[272,128]{1,0:T(8,128)S(1)} collective-permute-done((f32[272,128]{1,0:T(8,128)S(1)}, f32[272,128]{1,0:T(8,128)S(1)}, u32[]{:S(2)}, u32[]{:S(2)}) %collective-permute-start.7) | collective-permute-done | bytes 139296 | tf_op jit(solution)/shard_map/ppermute | solution.py:79
  428.8 3.9 collective-permute-done.8
  432.8 5.4 %collective-permute-done.9 = f32[272,128]{1,0:T(8,128)S(1)} collective-permute-done((f32[272,128]{1,0:T(8,128)S(1)}, f32[272,128]{1,0:T(8,128)S(1)}, u32[]{:S(2)}, u32[]{:S(2)}) %collective-permute-start.9) | collective-permute-done | bytes 139296 | tf_op jit(solution)/shard_map/ppermute | solution.py:79
  438.2 0.8 multiply_bitcast_fusion
  (44 shorter events, 1.5 us)
Async XLA Ops:
  7.2 165.2 %all-reduce.4.cloned.1.call-start = ((), (), s32[]{:S(2)}) async-start(), calls=%async_computation | async-start | bytes 557056 | tf_op jit(solution)/shard_map/pmax | solution.py:50
  10.2 162.2 %copy-start = (f32[34816]{0:T(1024)S(1)}, f32[34816]{0:T(1024)}, u32[]{:S(2)}) copy-start(f32[34816]{0:T(1024)} %param.20) | copy-start | bytes 417796
  10.2 164.4 %copy-start.1 = (f32[34816]{0:T(1024)S(1)}, f32[34816]{0:T(1024)}, u32[]{:S(2)}) copy-start(f32[34816]{0:T(1024)} %param.22) | copy-start | bytes 417796
  175.4 39.3 %copy-start.2 = (f32[8192]{0:T(1024)S(1)}, f32[8192]{0:T(1024)}, u32[]{:S(2)}) copy-start(f32[8192]{0:T(1024)} %param.17) | copy-start | bytes 98308
  175.4 134.2 %copy-start.3 = (f32[8192]{0:T(1024)S(1)}, f32[8192]{0:T(1024)}, u32[]{:S(2)}) copy-start(f32[8192]{0:T(1024)} %param.19) | copy-start | bytes 98308
  175.4 134.2 %copy-start.4 = (f32[8192]{0:T(1024)S(1)}, f32[8192]{0:T(1024)}, u32[]{:S(2)}) copy-start(f32[8192]{0:T(1024)} %param.18) | copy-start | bytes 98308
  175.4 134.2 %copy-start.5 = (f32[8192]{0:T(1024)S(1)}, f32[8192]{0:T(1024)}, u32[]{:S(2)}) copy-start(f32[8192]{0:T(1024)} %param.21) | copy-start | bytes 98308
  326.0 8.5 %collective-permute-start = (f32[272,128]{1,0:T(8,128)S(1)}, f32[272,128]{1,0:T(8,128)S(1)}, u32[]{:S(2)}, u32[]{:S(2)}) collective-permute-start(f32[272,128]{1,0:T(8,128)S(1)} %fusion.11), channel_id=1, source_target_pairs={{0,1},{1,0},{2,3},{3,2},{4,5},{5,4},{6,7},{7,6},{8,9},{9,8},{10,11... | collective-permute-start | bytes 417800 | tf_op jit(solution)/shard_map/ppermute | solution.py:79
  334.6 5.0 %collective-permute-start.1 = (f32[272,128]{1,0:T(8,128)S(1)}, f32[272,128]{1,0:T(8,128)S(1)}, u32[]{:S(2)}, u32[]{:S(2)}) collective-permute-start(f32[272,128]{1,0:T(8,128)S(1)} %add.92), channel_id=1, source_target_pairs={{0,2},{1,3},{2,0},{3,1},{4,6},{5,7},{6,4},{7,5},{8,10},{9,11},{10,... | collective-permute-start | bytes 417800 | tf_op jit(solution)/shard_map/ppermute | solution.py:79
  339.6 5.5 %collective-permute-start.2 = (f32[272,128]{1,0:T(8,128)S(1)}, f32[272,128]{1,0:T(8,128)S(1)}, u32[]{:S(2)}, u32[]{:S(2)}) collective-permute-start(f32[272,128]{1,0:T(8,128)S(1)} %add.93), channel_id=1, source_target_pairs={{0,4},{1,5},{2,6},{3,7},{4,0},{5,1},{6,2},{7,3},{8,12},{9,13},{10,... | collective-permute-start | bytes 417800 | tf_op jit(solution)/shard_map/ppermute | solution.py:79
  345.1 4.0 collective-permute-start.3
  349.1 5.7 %collective-permute-start.4 = (f32[272,128]{1,0:T(8,128)S(1)}, f32[272,128]{1,0:T(8,128)S(1)}, u32[]{:S(2)}, u32[]{:S(2)}) collective-permute-start(f32[272,128]{1,0:T(8,128)S(1)} %add.95), channel_id=1, source_target_pairs={{0,16},{1,17},{2,18},{3,19},{4,20},{5,21},{6,22},{7,23},{8,24},{9,... | collective-permute-start | bytes 417800 | tf_op jit(solution)/shard_map/ppermute | solution.py:79
  403.9 14.3 %collective-permute-start.5 = (f32[272,128]{1,0:T(8,128)S(1)}, f32[272,128]{1,0:T(8,128)S(1)}, u32[]{:S(2)}, u32[]{:S(2)}) collective-permute-start(f32[272,128]{1,0:T(8,128)S(1)} %fusion.9), channel_id=1, source_target_pairs={{0,1},{1,0},{2,3},{3,2},{4,5},{5,4},{6,7},{7,6},{8,9},{9,8},{10,11... | collective-permute-start | bytes 417800 | tf_op jit(solution)/shard_map/ppermute | solution.py:79
  418.2 5.0 %collective-permute-start.6 = (f32[272,128]{1,0:T(8,128)S(1)}, f32[272,128]{1,0:T(8,128)S(1)}, u32[]{:S(2)}, u32[]{:S(2)}) collective-permute-start(f32[272,128]{1,0:T(8,128)S(1)} %add.98), channel_id=1, source_target_pairs={{0,2},{1,3},{2,0},{3,1},{4,6},{5,7},{6,4},{7,5},{8,10},{9,11},{10,... | collective-permute-start | bytes 417800 | tf_op jit(solution)/shard_map/ppermute | solution.py:79
  423.2 5.5 %collective-permute-start.7 = (f32[272,128]{1,0:T(8,128)S(1)}, f32[272,128]{1,0:T(8,128)S(1)}, u32[]{:S(2)}, u32[]{:S(2)}) collective-permute-start(f32[272,128]{1,0:T(8,128)S(1)} %add.99), channel_id=1, source_target_pairs={{0,4},{1,5},{2,6},{3,7},{4,0},{5,1},{6,2},{7,3},{8,12},{9,13},{10,... | collective-permute-start | bytes 417800 | tf_op jit(solution)/shard_map/ppermute | solution.py:79
  428.7 4.0 collective-permute-start.8
  432.7 5.5 %collective-permute-start.9 = (f32[272,128]{1,0:T(8,128)S(1)}, f32[272,128]{1,0:T(8,128)S(1)}, u32[]{:S(2)}, u32[]{:S(2)}) collective-permute-start(f32[272,128]{1,0:T(8,128)S(1)} %add.101), channel_id=1, source_target_pairs={{0,16},{1,17},{2,18},{3,19},{4,20},{5,21},{6,22},{7,23},{8,24},{9,... | collective-permute-start | bytes 417800 | tf_op jit(solution)/shard_map/ppermute | solution.py:79
Sparse Core Ops, SparseCore 0:
  55.7 116.6 all-reduce.3
